TPU v7x, 256 devices: a whole 4x4x8 slice. The times are simulated.
256 devices in a mesh: dp: 16 (over y_hi, z), seq: 16 (over x, y_lo, core).
Axes of the slice: x: 4, y: 4 (y_hi: 2, y_lo: 2; y = y_hi * 2 + y_lo), z: 8, core: 2. Of those that a mesh axis runs over, the one named last changes fastest.
Arguments:
- queries: bfloat16 [16, 2048, 2048], P('dp', 'seq'), may hold values from -6 to 6
- key_states: bfloat16 [16, 2048, 2048], P('dp', 'seq'), may hold values from -6 to 6
- value_states: bfloat16 [16, 2048, 2048], P('dp', 'seq'), may hold values from -6 to 6
- cotangent: bfloat16 [16, 2048, 2048], P('dp', 'seq'), may hold values from -6 to 6
- filter_taps: float32 [7, 2048], replicated, may hold values from -3 to 3
Outputs:
- conv_output: bfloat16 [16, 2048, 2048], P('dp', 'seq')
- grad_queries: bfloat16 [16, 2048, 2048], P('dp', 'seq')
- grad_keys: bfloat16 [16, 2048, 2048], P('dp', 'seq')
- grad_values: bfloat16 [16, 2048, 2048], P('dp', 'seq')
- filter_gradient: float32 [7, 2048], replicated
All inputs are finite; a program needn't handle non-finite values.
Results may differ from a plain program's by a relative error of at most 0.015.
Values may be sent and summed in bfloat16 or wider, within the bound.
No kernel may reach another device: no remote copies, remote signals or barrier semaphores. Data moves between devices by JAX's collectives and lax.ppermute only.
A program may use at most 128 MiB of HBM per device.

v0:
```python
import jax
import jax.numpy as jnp
from jax import lax
from jax.sharding import PartitionSpec as P

HD = 128
TAPS = 7


def padded(value, width):
    peers = lax.axis_size("seq")
    length = value.shape[0]
    up = [(i, (i + 1) % peers) for i in range(peers)]
    down = [(j, i) for i, j in up]
    before = lax.ppermute(value[length - width :], "seq", up)
    after = lax.ppermute(value[:width], "seq", down)
    return jnp.concatenate([before, value, after], axis=0)


def butterfly_sum(value):
    axes = ("dp", "seq")
    peers = lax.axis_size("dp") * lax.axis_size("seq")
    bit = 1
    while bit < peers:
        pairs = [(i, i ^ bit) for i in range(peers)]
        value = value + lax.ppermute(value, axes, pairs)
        bit *= 2
    return value


def butterfly_gather(value):
    peers = lax.axis_size("seq")
    index = lax.axis_index("seq")
    bit = 1
    while bit < peers:
        pairs = [(i, i ^ bit) for i in range(peers)]
        other = lax.ppermute(value, "seq", pairs)
        upper = index & bit != 0
        value = jnp.where(
            upper, jnp.concatenate([other, value], axis=0), jnp.concatenate([value, other], axis=0)
        )
        bit *= 2
    return value


def on_device(queries, key_states, value_states, cotangent, filter_taps):
    tok_rows = queries.shape[1]
    channels = queries.shape[2]
    peers = lax.axis_size("seq")
    seq_total = tok_rows * peers
    head_count = channels // HD
    score_scale = HD ** (-0.5)
    half_width = (TAPS - 1) // 2
    local_q = queries[0]
    local_k = key_states[0]
    local_v = value_states[0]
    local_g = cotangent[0]
    grad_pad = padded(local_g, half_width)
    grad_sum = jnp.zeros((tok_rows, channels), jnp.float32)
    for tap_index in range(TAPS):
        start_row = 2 * half_width - tap_index
        grad_sum = grad_sum + filter_taps[tap_index] * grad_pad[
            start_row : start_row + tok_rows
        ].astype(jnp.float32)
    grad_attn = grad_sum.astype(jnp.bfloat16)

    def head_major(matrix):
        return matrix.reshape(tok_rows, head_count, HD).transpose(1, 0, 2)

    k_heads = lax.all_gather(head_major(local_k), "seq", axis=1, tiled=True)
    k_heads, local_v = lax.optimization_barrier((k_heads, local_v))
    v_heads = lax.all_gather(head_major(local_v), "seq", axis=1, tiled=True)
    q_heads = local_q.reshape(tok_rows, head_count, HD)
    d_heads = grad_attn.reshape(tok_rows, head_count, HD)
    device_index = lax.axis_index("seq")
    own_pos = device_index * tok_rows + jnp.arange(tok_rows, dtype=jnp.int32)
    all_pos = jnp.arange(seq_total, dtype=jnp.int32)
    visible = own_pos[:, None] >= all_pos[None, :]
    scores = (
        jnp.einsum("thd,hud->htu", q_heads, k_heads, preferred_element_type=jnp.float32)
        * score_scale
    )
    row_top = jnp.max(jnp.where(visible, scores, -jnp.inf), -1, keepdims=True)
    row_top, local_q2 = lax.optimization_barrier((row_top, local_q))
    qa_heads = lax.all_gather(head_major(local_q2), "seq", axis=1, tiled=True)
    raw = jnp.where(visible, jnp.exp(scores - row_top), 0.0)
    row_total = jnp.sum(raw, -1, keepdims=True)
    probs = raw / row_total
    probs_low = probs.astype(jnp.bfloat16)
    probs_low, grad_attn2 = lax.optimization_barrier((probs_low, grad_attn))
    da_heads = lax.all_gather(head_major(grad_attn2), "seq", axis=1, tiled=True)
    attended = jnp.einsum("htu,hud->thd", probs_low, v_heads, preferred_element_type=jnp.float32)
    attn_out = attended.astype(jnp.bfloat16).reshape(tok_rows, channels)
    dprob = jnp.einsum("thd,hud->htu", d_heads, v_heads, preferred_element_type=jnp.float32)
    row_delta = jnp.sum(probs * dprob, -1, keepdims=True)
    dscore = (probs * (dprob - row_delta) * score_scale).astype(jnp.bfloat16)
    grad_q = jnp.einsum("htu,hud->thd", dscore, k_heads, preferred_element_type=jnp.float32)
    grad_queries = grad_q.astype(jnp.bfloat16).reshape(tok_rows, channels)
    stats = jnp.stack([row_top[..., 0], row_total[..., 0], row_delta[..., 0]], 0)
    stats = butterfly_gather(stats.transpose(2, 0, 1)).transpose(1, 0, 2)
    top_all = stats[0].T[:, None, :]
    total_all = stats[1].T[:, None, :]
    delta_all = stats[2].T[:, None, :]
    kq_heads = head_major(local_k)
    kv_heads = head_major(local_v)
    key_visible = all_pos[None, :] >= own_pos[:, None]
    scores_t = (
        jnp.einsum("hud,htd->hut", kq_heads, qa_heads, preferred_element_type=jnp.float32)
        * score_scale
    )
    raw_t = jnp.where(key_visible, jnp.exp(scores_t - top_all), 0.0)
    probs_t = raw_t / total_all
    probs_low_t = probs_t.astype(jnp.bfloat16)
    dprob_t = jnp.einsum("hud,htd->hut", kv_heads, da_heads, preferred_element_type=jnp.float32)
    dscore_t = (probs_t * (dprob_t - delta_all) * score_scale).astype(jnp.bfloat16)
    grad_k = jnp.einsum("hut,htd->uhd", dscore_t, qa_heads, preferred_element_type=jnp.float32)
    grad_v = jnp.einsum("hut,htd->uhd", probs_low_t, da_heads, preferred_element_type=jnp.float32)
    grad_keys = grad_k.astype(jnp.bfloat16).reshape(tok_rows, channels)
    grad_values = grad_v.astype(jnp.bfloat16).reshape(tok_rows, channels)
    out_pad = padded(attn_out, half_width)
    conv_sum = jnp.zeros((tok_rows, channels), jnp.float32)
    filter_rows = []
    local_gf = local_g.astype(jnp.float32)
    for tap_index in range(TAPS):
        moved = out_pad[tap_index : tap_index + tok_rows].astype(jnp.float32)
        conv_sum = conv_sum + filter_taps[tap_index] * moved
        filter_rows.append(jnp.sum(moved * local_gf, 0))
    filter_gradient = butterfly_sum(jnp.stack(filter_rows, 0))
    conv_output = conv_sum.astype(jnp.bfloat16)
    return (
        conv_output[None],
        grad_queries[None],
        grad_keys[None],
        grad_values[None],
        filter_gradient,
    )


def solution(mesh):
    block = P("dp", "seq", None)
    in_specs = (block, block, block, block, P())
    out_specs = (block, block, block, block, P())
    return jax.shard_map(
        on_device, mesh=mesh, in_specs=in_specs, out_specs=out_specs, check_vma=False
    )
```

profile of v0, /device:TPU:1, one launch (start us, length us, event | category | flops | bytes accessed | tf_op | source)
XLA Modules:
  0.0 298.4 jit_solution(1885777955495145412)
XLA Ops:
  10.7 58.6 %all-gather.5.cloned.1.call-done = bf16[16,2048,128]{2,1,0:T(8,128)(2,1)} async-done(((bf16[16,128,128]{2,1,0:T(8,128)(2,1)}), bf16[16,2048,128]{2,1,0:T(8,128)(2,1)}) %all-gather.5.cloned.1.call-update) | async-done | bytes 8388624 | tf_op jit(solution)/shard_map/all_gather | solution.py:70
  73.9 11.8 %fusion.1 = (f32[16,128]{1,0:T(8,128)S(1)}, f32[16,2048,128]{2,1,0:T(8,128)}) fusion(pred[128,2048]{0,1:T(8,128)(4,1)S(1)} %get-tuple-element.63, bf16[16,2048,128]{2,1,0:T(8,128)(2,1)} %all-gather.5.cloned.1.call-done, bf16[128,16,128]{2,1,0:T(8,128)(2,1)S(1)} %bitcast.140), kind=kOutput, calls=%fused_computation.4 | convolution fusion | flops 1086322688 | bytes 25960448 | tf_op jit(solution)/shard_map/thd,hud->htu/dot_general | solution.py:80
  89.2 22.3 %collective-permute-done.1 = bf16[3,2048]{0,1:T(8,128)(2,1)S(1)} collective-permute-done((bf16[3,2048]{0,1:T(8,128)(2,1)S(1)}, bf16[3,2048]{0,1:T(8,128)(2,1)S(1)}, u32[]{:S(2)}, u32[]{:S(2)}) %collective-permute-start.1) | collective-permute-done | bytes 12320 | tf_op jit(solution)/shard_map/ppermute | solution.py:15
  111.5 3.4 %collective-permute-done = bf16[3,2048]{0,1:T(8,128)(2,1)S(1)} collective-permute-done((bf16[3,2048]{0,1:T(8,128)(2,1)S(1)}, bf16[3,2048]{0,1:T(8,128)(2,1)S(1)}, u32[]{:S(2)}, u32[]{:S(2)}) %collective-permute-start) | collective-permute-done | bytes 12320 | tf_op jit(solution)/shard_map/ppermute | solution.py:16
  114.9 3.7 %fusion.33 = bf16[128,2048]{0,1:T(8,128)(2,1)S(1)} fusion(bf16[128,2048]{0,1:T(8,128)(2,1)S(1)} %bitcast.122, bf16[3,2048]{0,1:T(8,128)(2,1)S(1)} %collective-permute-done.1, bf16[3,2048]{0,1:T(8,128)(2,1)S(1)} %collective-permute-done, f32[2048]{0:T(1024)S(1)} %bitcast.152, f32[2048]{0:T(1024)S(1)} %bitcast.154, f32[2048]{0:T(1024)S(1)} %bitcast.144, ...), kind=kLoop, calls=%fused_computation.66 | loop fusion | flops 10223616 | bytes 1130496 | tf_op jit(solution)/shard_map/convert_element_type | solution.py:65
  118.7 9.5 %fusion.5 = f32[16,128]{1,0:T(8,128)S(1)} fusion(f32[16,2048,128]{2,1,0:T(8,128)} %get-tuple-element.65, f32[16,128]{1,0:T(8,128)S(1)} %get-tuple-element.64, pred[128,2048]{0,1:T(8,128)(4,1)S(1)} %get-tuple-element.63), kind=kLoop, calls=%fused_computation.11 | loop fusion | flops 16775168 | bytes 17055744 | tf_op jit(solution)/shard_map/reduce_sum | solution.py:87
  128.2 10.3 %all-gather.7.cloned.1.call-done = bf16[16,2048,128]{2,1,0:T(8,128)(2,1)} async-done(((bf16[16,128,128]{2,1,0:T(8,128)(2,1)}), bf16[16,2048,128]{2,1,0:T(8,128)(2,1)}) %all-gather.7.cloned.1.call-update) | async-done | bytes 8388624 | tf_op jit(solution)/shard_map/all_gather | solution.py:72
  138.5 16.0 %multiply_reduce_fusion = (f32[16,128]{1,0:T(8,128)S(1)}, bf16[16,128,2048]{1,2,0:T(8,128)(2,1)}, f32[16,128,2048]{1,2,0:T(8,128)}) fusion(f32[16,128]{1,0:T(8,128)S(1)} %fusion.5, f32[16,128]{1,0:T(8,128)S(1)} %get-tuple-element.64, f32[16,2048,128]{2,1,0:T(8,128)} %get-tuple-element.65, pred[128,2048]{0,1:T(8,128)(4,1)S(1)} %get-tuple-element.63, ...), kind=kOutput, calls=%fused_computation.9 | convolution fusion | flops 1103099904 | bytes 51142656 | tf_op jit(solution)/shard_map/thd,hud->htu/dot_general | solution.py:94
  155.7 8.8 %multiply_reduce_fusion.1 = (f32[16,128]{1,0:T(8,128)S(1)}, bf16[128,16,128]{2,0,1:T(8,128)(2,1)S(1)}) fusion(f32[128,16,128]{2,0,1:T(8,128)S(1)} %copy.104, bf16[16,2048,128]{2,1,0:T(8,128)(2,1)} %all-gather.7.cloned.1.call-done, bf16[16,128,2048]{1,2,0:T(8,128)(2,1)} %get-tuple-element.14), kind=kOutput, calls=%fused_computation.73 | convolution fusion | flops 1074788352 | bytes 18358272 | tf_op jit(solution)/shard_map/htu,hud->thd/dot_general | solution.py:92
  166.9 19.5 %collective-permute-done.3 = bf16[3,2048]{0,1:T(8,128)(2,1)S(1)} collective-permute-done((bf16[3,2048]{0,1:T(8,128)(2,1)}, bf16[3,2048]{0,1:T(8,128)(2,1)S(1)}, u32[]{:S(2)}, u32[]{:S(2)}) %collective-permute-start.3) | collective-permute-done | bytes 12320 | tf_op jit(solution)/shard_map/ppermute | solution.py:16
  186.4 3.4 %fusion.39 = (f32[2048]{0:T(1024)S(1)}, f32[2048]{0:T(1024)S(1)}, f32[2048]{0:T(1024)S(1)}, f32[2048]{0:T(1024)S(1)}, f32[2048]{0:T(1024)S(1)}, /*index=5*/f32[2048]{0:T(1024)S(1)}) fusion(bf16[3,2048]{0,1:T(8,128)(2,1)S(1)} %collective-permute-done.3, bf16[128,2048]{0,1:T(8,128)(2,1)S(1)} %bitcast.125, bf16[1,128,2048]{1,2,0:T(8,128)(2,1)S(1)} %copy.84, ...), kind=kLoop, calls=%fused_computation.72 | loop fusion | flops 9687040 | bytes 1122304 | tf_op jit(solution)/shard_map/reduce_sum | solution.py:127
  193.0 3.8 %collective-permute-done.9 = f32[7,2048]{1,0:T(8,128)S(1)} collective-permute-done((f32[7,2048]{1,0:T(8,128)S(1)}, f32[7,2048]{1,0:T(8,128)S(1)}, u32[]{:S(2)}, u32[]{:S(2)}) %collective-permute-start.9) | collective-permute-done | bytes 57376 | tf_op jit(solution)/shard_map/ppermute | solution.py:26
  196.9 2.0 collective-permute-done.5
  200.4 2.4 collective-permute-start.11
  202.8 17.1 %fusion.20 = bf16[16,128,128]{2,1,0:T(8,128)(2,1)S(1)} fusion(bf16[16,2048,128]{2,1,0:T(8,128)(2,1)} %all-gather.5.cloned.1.call-done, f32[16,128,2048]{1,2,0:T(8,128)} %get-tuple-element.66, f32[16,128]{1,0:T(8,128)S(1)} %get-tuple-element.46, f32[16,2048,128]{2,1,0:T(8,128)} %get-tuple-element.65, f32[16,128]{1,0:T(8,128)S(1)} %fusion.5, ...), kind=kOutput, calls=%fused_computation.37 | convolution fusion | flops 1107558400 | bytes 42754048 | tf_op jit(solution)/shard_map/htu,hud->thd/dot_general | solution.py:97
  224.5 2.6 collective-permute-start.13
  227.1 3.7 %fusion.50 = bf16[1,128,2048]{1,2,0:T(8,128)(2,1)S(1)} fusion(f32[2048]{0:T(1024)S(1)} %bitcast.153, f32[2048]{0:T(1024)S(1)} %bitcast.155, f32[2048]{0:T(1024)S(1)} %bitcast.145, bf16[128,2048]{0,1:T(8,128)(2,1)S(1)} %bitcast.126, f32[2048]{0:T(1024)S(1)} %bitcast.147, f32[2048]{0:T(1024)S(1)} %bitcast.149, f32[2048]{0:T(1024)S(1)} %bitcast.151, ...), kind=kLoop, calls=%fused_computation.93 | loop fusion | flops 10223616 | bytes 1130496 | tf_op jit(solution)/shard_map/broadcast_in_dim | solution.py:131
  231.8 3.7 %collective-permute-start.14 = (f32[7,2048]{1,0:T(8,128)S(1)}, f32[7,2048]{1,0:T(8,128)S(1)}, u32[]{:S(2)}, u32[]{:S(2)}) collective-permute-start(f32[7,2048]{1,0:T(8,128)S(1)} %add.89), channel_id=1, source_target_pairs={{0,64},{1,65},{2,66},{3,67},{4,68},{5,69},{6,70},{7,71},{8,72},{9,... | collective-permute-start | bytes 172040 | tf_op jit(solution)/shard_map/ppermute | solution.py:26
  235.6 3.3 %collective-permute-done.14 = f32[7,2048]{1,0:T(8,128)S(1)} collective-permute-done((f32[7,2048]{1,0:T(8,128)S(1)}, f32[7,2048]{1,0:T(8,128)S(1)}, u32[]{:S(2)}, u32[]{:S(2)}) %collective-permute-start.14) | collective-permute-done | bytes 57376 | tf_op jit(solution)/shard_map/ppermute | solution.py:26
  238.9 2.7 collective-permute-start.15
  241.6 15.0 %fusion = f32[16,128,2048]{1,2,0:T(8,128)} fusion(f32[16,2048]{1,0:T(8,128)S(1)} %get-tuple-element.53, f32[16,2048]{1,0:T(8,128)S(1)} %get-tuple-element.54, pred[128,2048]{0,1:T(8,128)(4,1)} %get-tuple-element.62, bf16[16,2048,128]{2,1,0:T(8,128)(2,1)} %all-gather.9.cloned.1.call-done, bf16[128,16,128]{2,1,0:T(8,128)(2,1)S(1)} %bitcast.131), kind=kOutput, calls=%fused_computation.1 | convolution fusion | flops 1090519040 | bytes 26214400 | tf_op jit(solution)/shard_map/hud,htd->hut/dot_general | solution.py:108
  257.2 7.9 %all-gather.11.cloned.1.call-done = bf16[16,2048,128]{2,1,0:T(8,128)(2,1)} async-done(((bf16[16,128,128]{2,1,0:T(8,128)(2,1)}), bf16[16,2048,128]{2,1,0:T(8,128)(2,1)}) %all-gather.11.cloned.1.call-update) | async-done | bytes 8388624 | tf_op jit(solution)/shard_map/all_gather | solution.py:91
  265.2 13.5 %fusion.19 = bf16[16,128,128]{2,1,0:T(8,128)(2,1)S(1)} fusion(bf16[16,2048,128]{2,1,0:T(8,128)(2,1)} %all-gather.9.cloned.1.call-done, f32[16,128,2048]{1,2,0:T(8,128)} %fusion, f32[16,2048]{1,0:T(8,128)S(1)} %get-tuple-element.52, bf16[16,2048,128]{2,1,0:T(8,128)(2,1)} %all-gather.11.cloned.1.call-done, bf16[128,16,128]{2,0,1:T(8,128)(2,1)S(1)} %copy-done), kind=kOutput, calls=%fused_computation.35 | convolution fusion | flops 2164523008 | bytes 34734080 | tf_op jit(solution)/shard_map/hut,htd->uhd/dot_general | solution.py:116
  279.7 10.9 %fusion.16 = bf16[16,128,128]{2,1,0:T(8,128)(2,1)S(1)} fusion(bf16[16,2048,128]{2,1,0:T(8,128)(2,1)} %all-gather.11.cloned.1.call-done, f32[16,128,2048]{1,2,0:T(8,128)} %fusion), kind=kOutput, calls=%fused_computation.34 | convolution fusion | flops 1078198272 | bytes 25690112 | tf_op jit(solution)/shard_map/hut,htd->uhd/dot_general | solution.py:117
  (74 shorter events, 28.2 us)
Async XLA Ops:
  7.2 62.1 %all-gather.5.cloned.1.call-start = ((), (), s32[]{:S(2)}) async-start(), calls=%async_computation | async-start | bytes 8912896 | tf_op jit(solution)/shard_map/all_gather | solution.py:70
  9.3 129.2 %all-gather.7.cloned.1.call-start = ((), (), s32[]{:S(2)}) async-start(), calls=%async_computation.1 | async-start | bytes 8912896 | tf_op jit(solution)/shard_map/all_gather | solution.py:72
  70.3 171.3 %all-gather.9.cloned.1.call-start = ((), (), s32[]{:S(2)}) async-start(), calls=%async_computation.2 | async-start | bytes 8912896 | tf_op jit(solution)/shard_map/all_gather | solution.py:85
  73.9 12.9 %copy-start.1 = (bf16[1,128,2048]{2,1,0:T(8,128)(2,1)S(1)}, bf16[1,128,2048]{2,1,0:T(8,128)(2,1)}, u32[]{:S(2)}) copy-start(bf16[1,128,2048]{2,1,0:T(8,128)(2,1)} %param.8) | copy-start | bytes 1572868
  73.9 15.3 %copy-start.2 = (f32[7,2048]{1,0:T(8,128)S(1)}, f32[7,2048]{1,0:T(8,128)}, u32[]{:S(2)}) copy-start(f32[7,2048]{1,0:T(8,128)} %param.9) | copy-start | bytes 172036
  86.7 178.4 %all-gather.11.cloned.1.call-start = ((), (), s32[]{:S(2)}) async-start(), calls=%async_computation.3 | async-start | bytes 8912896 | tf_op jit(solution)/shard_map/all_gather | solution.py:91
  87.3 24.3 %collective-permute-start.1 = (bf16[3,2048]{0,1:T(8,128)(2,1)S(1)}, bf16[3,2048]{0,1:T(8,128)(2,1)S(1)}, u32[]{:S(2)}, u32[]{:S(2)}) collective-permute-start(bf16[3,2048]{0,1:T(8,128)(2,1)S(1)} %get-tuple-element.51), channel_id=1, source_target_pairs={{0,1},{1,2},{2,3},{3,4},{4,5},{5,6},{6,7},{7,8},{8,9},{9,10},{10,1... | collective-permute-start | bytes 36872 | tf_op jit(solution)/shard_map/ppermute | solution.py:15
  88.7 26.3 %collective-permute-start = (bf16[3,2048]{0,1:T(8,128)(2,1)S(1)}, bf16[3,2048]{0,1:T(8,128)(2,1)S(1)}, u32[]{:S(2)}, u32[]{:S(2)}) collective-permute-start(bf16[3,2048]{0,1:T(8,128)(2,1)S(1)} %get-tuple-element.50), channel_id=1, source_target_pairs={{1,0},{2,1},{3,2},{4,3},{5,4},{6,5},{7,6},{8,7},{9,8},{10,9},{11,1... | collective-permute-start | bytes 36872 | tf_op jit(solution)/shard_map/ppermute | solution.py:16
  164.5 2.1 collective-permute-start.2
  165.7 20.7 %collective-permute-start.3 = (bf16[3,2048]{0,1:T(8,128)(2,1)}, bf16[3,2048]{0,1:T(8,128)(2,1)S(1)}, u32[]{:S(2)}, u32[]{:S(2)}) collective-permute-start(bf16[3,2048]{0,1:T(8,128)(2,1)} %copy.90), channel_id=1, source_target_pairs={{1,0},{2,1},{3,2},{4,3},{5,4},{6,5},{7,6},{8,7},{9,8},{10,9},{11,1... | collective-permute-start | bytes 36872 | tf_op jit(solution)/shard_map/ppermute | solution.py:16
  189.9 1.3 collective-permute-start.8
  190.1 1.6 collective-permute-start.4
  191.3 5.5 %collective-permute-start.9 = (f32[7,2048]{1,0:T(8,128)S(1)}, f32[7,2048]{1,0:T(8,128)S(1)}, u32[]{:S(2)}, u32[]{:S(2)}) collective-permute-start(f32[7,2048]{1,0:T(8,128)S(1)} %add.84), channel_id=1, source_target_pairs={{0,2},{1,3},{2,0},{3,1},{4,6},{5,7},{6,4},{7,5},{8,10},{9,11},{10,... | collective-permute-start | bytes 172040 | tf_op jit(solution)/shard_map/ppermute | solution.py:26
  191.6 7.3 %collective-permute-start.5 = (f32[256,3,16]{0,2,1:T(8,128)S(1)}, f32[256,3,16]{0,2,1:T(8,128)S(1)}, u32[]{:S(2)}, u32[]{:S(2)}) collective-permute-start(f32[256,3,16]{0,2,1:T(8,128)S(1)} %maximum_select_fusion.3), channel_id=1, source_target_pairs={{0,2},{1,3},{2,0},{3,1},{4,6},{5,7},{6,4},{7,5},{8,10},{9,11},{10,... | collective-permute-start | bytes 147464 | tf_op jit(solution)/shard_map/ppermute | solution.py:37
  196.8 3.6 %collective-permute-start.10 = (f32[7,2048]{1,0:T(8,128)S(1)}, f32[7,2048]{1,0:T(8,128)S(1)}, u32[]{:S(2)}, u32[]{:S(2)}) collective-permute-start(f32[7,2048]{1,0:T(8,128)S(1)} %add.85), channel_id=1, source_target_pairs={{0,4},{1,5},{2,6},{3,7},{4,0},{5,1},{6,2},{7,3},{8,12},{9,13},{10,... | collective-permute-start | bytes 172040 | tf_op jit(solution)/shard_map/ppermute | solution.py:26
  198.9 23.3 %collective-permute-start.6 = (f32[512,3,16]{0,2,1:T(8,128)S(1)}, f32[512,3,16]{0,2,1:T(8,128)S(1)}, u32[]{:S(2)}, u32[]{:S(2)}) collective-permute-start(f32[512,3,16]{0,2,1:T(8,128)S(1)} %maximum_select_fusion.2), channel_id=1, source_target_pairs={{0,4},{1,5},{2,6},{3,7},{4,0},{5,1},{6,2},{7,3},{8,12},{9,13},{10,... | collective-permute-start | bytes 294920 | tf_op jit(solution)/shard_map/ppermute | solution.py:37
  200.4 20.4 %collective-permute-start.11 = (f32[7,2048]{1,0:T(8,128)S(1)}, f32[7,2048]{1,0:T(8,128)S(1)}, u32[]{:S(2)}, u32[]{:S(2)}) collective-permute-start(f32[7,2048]{1,0:T(8,128)S(1)} %add.86), channel_id=1, source_target_pairs={{0,8},{1,9},{2,10},{3,11},{4,12},{5,13},{6,14},{7,15},{8,0},{9,1},... | collective-permute-start | bytes 172040 | tf_op jit(solution)/shard_map/ppermute | solution.py:26
  220.9 3.6 %collective-permute-start.12 = (f32[7,2048]{1,0:T(8,128)S(1)}, f32[7,2048]{1,0:T(8,128)S(1)}, u32[]{:S(2)}, u32[]{:S(2)}) collective-permute-start(f32[7,2048]{1,0:T(8,128)S(1)} %add.87), channel_id=1, source_target_pairs={{0,16},{1,17},{2,18},{3,19},{4,20},{5,21},{6,22},{7,23},{8,24},{9,... | collective-permute-start | bytes 172040 | tf_op jit(solution)/shard_map/ppermute | solution.py:26
  222.3 13.3 %collective-permute-start.7 = (f32[1024,3,16]{0,2,1:T(8,128)S(1)}, f32[1024,3,16]{0,2,1:T(8,128)S(1)}, u32[]{:S(2)}, u32[]{:S(2)}) collective-permute-start(f32[1024,3,16]{0,2,1:T(8,128)S(1)} %maximum_select_fusion.1), channel_id=1, source_target_pairs={{0,8},{1,9},{2,10},{3,11},{4,12},{5,13},{6,14},{7,15},{8,0},{9,1},... | collective-permute-start | bytes 589832 | tf_op jit(solution)/shard_map/ppermute | solution.py:37
  224.5 7.3 %collective-permute-start.13 = (f32[7,2048]{1,0:T(8,128)S(1)}, f32[7,2048]{1,0:T(8,128)S(1)}, u32[]{:S(2)}, u32[]{:S(2)}) collective-permute-start(f32[7,2048]{1,0:T(8,128)S(1)} %add.88), channel_id=1, source_target_pairs={{0,32},{1,33},{2,34},{3,35},{4,36},{5,37},{6,38},{7,39},{8,40},{9,... | collective-permute-start | bytes 172040 | tf_op jit(solution)/shard_map/ppermute | solution.py:26
  231.8 7.1 %collective-permute-start.14 = (f32[7,2048]{1,0:T(8,128)S(1)}, f32[7,2048]{1,0:T(8,128)S(1)}, u32[]{:S(2)}, u32[]{:S(2)}) collective-permute-start(f32[7,2048]{1,0:T(8,128)S(1)} %add.89), channel_id=1, source_target_pairs={{0,64},{1,65},{2,66},{3,67},{4,68},{5,69},{6,70},{7,71},{8,72},{9,... | collective-permute-start | bytes 172040 | tf_op jit(solution)/shard_map/ppermute | solution.py:26
  238.9 17.6 %collective-permute-start.15 = (f32[7,2048]{1,0:T(8,128)S(1)}, f32[7,2048]{1,0:T(8,128)S(1)}, u32[]{:S(2)}, u32[]{:S(2)}) collective-permute-start(f32[7,2048]{1,0:T(8,128)S(1)} %add.90), channel_id=1, source_target_pairs={{0,128},{1,129},{2,130},{3,131},{4,132},{5,133},{6,134},{7,135},{8... | collective-permute-start | bytes 172040 | tf_op jit(solution)/shard_map/ppermute | solution.py:26
  241.6 23.6 %copy-start = (bf16[128,16,128]{2,0,1:T(8,128)(2,1)S(1)}, bf16[128,16,128]{2,0,1:T(8,128)(2,1)}, u32[]{:S(2)}) copy-start(bf16[128,16,128]{2,0,1:T(8,128)(2,1)} %copy.81) | copy-start | bytes 1572868
Sparse Core Ops, SparseCore 0:
  10.4 58.8 all-gather.4
  71.7 66.7 all-gather.6
  140.3 63.5 all-gather.8
  205.5 59.5 all-gather.10
where the time goes:
time: 304 us; the launch traced here: 298 us
  waiting for transfers between devices  135 us (44%)
  matrix products  93 us (31%)
  other arithmetic  22.1 us (7%)
  starting transfers between devices  18.8 us (6%)
  local copies, waits for them, and re-layouts  15.5 us (5%)
  between operations  14.3 us (5%)
    all_gather x1, waiting for transfers between devices, on_device(): k_heads = lax.all_gather(head_major(local_k), 'seq', axis=1, tiled=True)  58.6 us
    ppermute x2, waiting for transfers between devices, padded(): after = lax.ppermute(value[:width], 'seq', down)  22.9 us
    ppermute x2, waiting for transfers between devices, padded(): before = lax.ppermute(value[length - width:], 'seq', up)  22.3 us
    dot_general x1, matrix products, on_device(): jnp.einsum('htu,hud->thd', dscore, k_heads, preferred_element_type=jnp.fl...  17.1 us
    dot_general x1, matrix products, on_device(): jnp.einsum('thd,hud->htu', d_heads, v_heads, preferred_element_type=jnp.f...  16 us
    dot_general x1, matrix products, on_device(): jnp.einsum('hud,htd->hut', kq_heads, qa_heads, preferred_element_type=jnp...  15 us
    dot_general x1, matrix products, on_device(): jnp.einsum('hut,htd->uhd', dscore_t, qa_heads, preferred_element_type=jnp...  13.5 us
    ppermute x8, starting transfers between devices, butterfly_sum(): value = value + lax.ppermute(value, axes, pairs)  13.2 us
  transfers between devices with their start and end apart: 20, of which 12 were waited for; matrix products, arithmetic and copies ran while one was open for 34% of the time, Pallas kernels for 0%

commit v1 on v0

--- a/solution.py
+++ b/solution.py
@@ -88,7 +88,11 @@
     probs = raw / row_total
     probs_low = probs.astype(jnp.bfloat16)
     probs_low, grad_attn2 = lax.optimization_barrier((probs_low, grad_attn))
-    da_heads = lax.all_gather(head_major(grad_attn2), "seq", axis=1, tiled=True)
+    block_2 = head_major(grad_attn2)
+    peers_2 = lax.axis_size("seq")
+    blocks = jnp.stack([block_2 for _ in range(peers_2)])
+    blocks = lax.all_to_all(blocks, "seq", split_axis=0, concat_axis=0)
+    da_heads = jnp.concatenate(blocks, axis=1)
     attended = jnp.einsum("htu,hud->thd", probs_low, v_heads, preferred_element_type=jnp.float32)
     attn_out = attended.astype(jnp.bfloat16).reshape(tok_rows, channels)
     dprob = jnp.einsum("thd,hud->htu", d_heads, v_heads, preferred_element_type=jnp.float32)

time: 304 us -> 437 us (1.44)
  the two profiles are of different devices: /device:TPU:1 before, /device:TPU:6 now
where the time goes in v1:
time: 437 us; the launch traced here: 431 us
  waiting for transfers between devices  207 us (47%)
  matrix products  92.7 us (21%)
  starting transfers between devices  58 us (13%)
  local copies, waits for them, and re-layouts  31.2 us (7%)
  other arithmetic  27.8 us (6%)
  between operations  14.2 us (3%)
    ppermute x8, waiting for transfers between devices, butterfly_sum(): value = value + lax.ppermute(value, axes, pairs)  110 us
    all_gather x1, waiting for transfers between devices, on_device(): k_heads = lax.all_gather(head_major(local_k), 'seq', axis=1, tiled=True)  57.2 us
    ppermute x8, starting transfers between devices, butterfly_sum(): value = value + lax.ppermute(value, axes, pairs)  40.4 us
    ppermute x2, waiting for transfers between devices, padded(): before = lax.ppermute(value[length - width:], 'seq', up)  17.7 us
    dot_general x1, matrix products, on_device(): jnp.einsum('htu,hud->thd', dscore, k_heads, preferred_element_type=jnp.fl...  17.1 us
    dot_general x1, matrix products, on_device(): jnp.einsum('thd,hud->htu', d_heads, v_heads, preferred_element_type=jnp.f...  16 us
    dot_general x1, matrix products, on_device(): jnp.einsum('hud,htd->hut', kq_heads, qa_heads, preferred_element_type=jnp...  14.8 us
    all_gather x1, waiting for transfers between devices, on_device(): v_heads = lax.all_gather(head_major(local_v), 'seq', axis=1, tiled=True)  14.2 us
  transfers between devices with their start and end apart: 20, of which 11 were waited for; matrix products, arithmetic and copies ran while one was open for 26% of the time, Pallas kernels for 0%

profile of v1, /device:TPU:6, one launch (start us, length us, event | category | flops | bytes accessed | tf_op | source)
XLA Modules:
  0.0 431.1 jit_solution(1909299309948894390)
XLA Ops:
  10.7 57.2 %all-gather.4.cloned.1.call-done = bf16[16,2048,128]{2,1,0:T(8,128)(2,1)} async-done(((bf16[16,128,128]{2,1,0:T(8,128)(2,1)}), bf16[16,2048,128]{2,1,0:T(8,128)(2,1)}) %all-gather.4.cloned.1.call-update) | async-done | bytes 8388624 | tf_op jit(solution)/shard_map/all_gather | solution.py:70
  72.5 11.8 %fusion.1 = (f32[16,128]{1,0:T(8,128)S(1)}, f32[16,2048,128]{2,1,0:T(8,128)}) fusion(pred[128,2048]{0,1:T(8,128)(4,1)S(1)} %get-tuple-element.63, bf16[16,2048,128]{2,1,0:T(8,128)(2,1)} %all-gather.4.cloned.1.call-done, bf16[128,16,128]{2,1,0:T(8,128)(2,1)S(1)} %bitcast.144), kind=kOutput, calls=%fused_computation.4 | convolution fusion | flops 1086322688 | bytes 25960448 | tf_op jit(solution)/shard_map/thd,hud->htu/dot_general | solution.py:80
  89.8 17.7 %collective-permute-done.1 = bf16[3,2048]{0,1:T(8,128)(2,1)S(1)} collective-permute-done((bf16[3,2048]{0,1:T(8,128)(2,1)}, bf16[3,2048]{0,1:T(8,128)(2,1)S(1)}, u32[]{:S(2)}, u32[]{:S(2)}) %collective-permute-start.1) | collective-permute-done | bytes 12320 | tf_op jit(solution)/shard_map/ppermute | solution.py:15
  107.6 5.9 %fusion.33 = bf16[128,2048]{0,1:T(8,128)(2,1)S(1)} fusion(bf16[128,2048]{0,1:T(8,128)(2,1)S(1)} %bitcast.128, bf16[3,2048]{0,1:T(8,128)(2,1)S(1)} %collective-permute-done.1, bf16[3,2048]{0,1:T(8,128)(2,1)} %collective-permute-done, f32[2048]{0:T(1024)S(1)} %bitcast.156, f32[2048]{0:T(1024)S(1)} %bitcast.158, f32[2048]{0:T(1024)S(1)} %bitcast.148, ...), kind=kLoop, calls=%fused_computation.66 | loop fusion | flops 10223616 | bytes 1130496 | tf_op jit(solution)/shard_map/convert_element_type | solution.py:65
  113.4 9.5 %fusion.5 = f32[16,128]{1,0:T(8,128)S(1)} fusion(f32[16,2048,128]{2,1,0:T(8,128)} %get-tuple-element.65, f32[16,128]{1,0:T(8,128)S(1)} %get-tuple-element.64, pred[128,2048]{0,1:T(8,128)(4,1)S(1)} %get-tuple-element.63), kind=kLoop, calls=%fused_computation.11 | loop fusion | flops 16775168 | bytes 17055744 | tf_op jit(solution)/shard_map/reduce_sum | solution.py:87
  122.9 14.2 %all-gather.6.cloned.1.call-done = bf16[16,2048,128]{2,1,0:T(8,128)(2,1)} async-done(((bf16[16,128,128]{2,1,0:T(8,128)(2,1)}), bf16[16,2048,128]{2,1,0:T(8,128)(2,1)}) %all-gather.6.cloned.1.call-update) | async-done | bytes 8388624 | tf_op jit(solution)/shard_map/all_gather | solution.py:72
  137.1 16.0 %multiply_reduce_fusion = (f32[16,128]{1,0:T(8,128)S(1)}, bf16[16,128,2048]{1,2,0:T(8,128)(2,1)}, f32[16,128,2048]{1,2,0:T(8,128)}) fusion(f32[16,128]{1,0:T(8,128)S(1)} %fusion.5, f32[16,128]{1,0:T(8,128)S(1)} %get-tuple-element.64, f32[16,2048,128]{2,1,0:T(8,128)} %get-tuple-element.65, pred[128,2048]{0,1:T(8,128)(4,1)S(1)} %get-tuple-element.63, ...), kind=kOutput, calls=%fused_computation.9 | convolution fusion | flops 1103099904 | bytes 51142656 | tf_op jit(solution)/shard_map/thd,hud->htu/dot_general | solution.py:98
  153.1 8.6 %multiply_reduce_fusion.1 = (f32[16,128]{1,0:T(8,128)S(1)}, bf16[128,16,128]{2,0,1:T(8,128)(2,1)S(1)}) fusion(f32[128,16,128]{2,0,1:T(8,128)S(1)} %copy.106, bf16[16,2048,128]{2,1,0:T(8,128)(2,1)} %all-gather.6.cloned.1.call-done, bf16[16,128,2048]{1,2,0:T(8,128)(2,1)} %get-tuple-element.14), kind=kOutput, calls=%fused_computation.73 | convolution fusion | flops 1074788352 | bytes 18358272 | tf_op jit(solution)/shard_map/htu,hud->thd/dot_general | solution.py:96
  166.6 5.3 %stack.21 = bf16[16,16,128,128]{3,2,1,0:T(8,128)(2,1)} broadcast(bf16[16,128,128]{2,1,0:T(8,128)(2,1)S(1)} %copy.98), dimensions={1,2,3} | broadcast | bytes 8912896 | tf_op jit(solution)/shard_map/stack | solution.py:93
  172.0 6.4 %all-to-all-start = ((bf16[16,16,128,128]{3,2,1,0:T(8,128)(2,1)}), bf16[16,16,128,128]{3,2,1,0:T(8,128)(2,1)}, u32[]{:S(2)}, u32[]{:S(2)}) async-start(bf16[16,16,128,128]{3,2,1,0:T(8,128)(2,1)} %stack.21), calls=%async_computation | async-start | bytes 16777216 | tf_op jit(solution)/shard_map/all_to_all | solution.py:94
  178.7 7.3 %collective-permute-done.3 = bf16[3,2048]{0,1:T(8,128)(2,1)} collective-permute-done((bf16[3,2048]{0,1:T(8,128)(2,1)}, bf16[3,2048]{0,1:T(8,128)(2,1)}, u32[]{:S(2)}, u32[]{:S(2)}) %collective-permute-start.3) | collective-permute-done | bytes 12320 | tf_op jit(solution)/shard_map/ppermute | solution.py:16
  186.0 4.8 %fusion.39 = (f32[2048]{0:T(1024)S(1)}, f32[2048]{0:T(1024)S(1)}, f32[2048]{0:T(1024)S(1)}, f32[2048]{0:T(1024)S(1)}, f32[2048]{0:T(1024)S(1)}, /*index=5*/f32[2048]{0:T(1024)S(1)}) fusion(bf16[3,2048]{0,1:T(8,128)(2,1)} %collective-permute-done.3, bf16[128,2048]{0,1:T(8,128)(2,1)S(1)} %bitcast.130, bf16[1,128,2048]{1,2,0:T(8,128)(2,1)S(1)} %copy.85, ...), kind=kLoop, calls=%fused_computation.72 | loop fusion | flops 9687040 | bytes 1122304 | tf_op jit(solution)/shard_map/reduce_sum | solution.py:131
  190.9 21.9 %collective-permute-start.8 = (f32[7,2048]{1,0:T(8,128)S(1)}, f32[7,2048]{1,0:T(8,128)S(1)}, u32[]{:S(2)}, u32[]{:S(2)}) collective-permute-start(f32[7,2048]{1,0:T(8,128)S(1)} %stack.55), channel_id=1, source_target_pairs={{0,1},{1,0},{2,3},{3,2},{4,5},{5,4},{6,7},{7,6},{8,9},{9,8},{10,11... | collective-permute-start | bytes 172040 | tf_op jit(solution)/shard_map/ppermute | solution.py:26
  215.9 72.0 %collective-permute-done.9 = f32[7,2048]{1,0:T(8,128)S(1)} collective-permute-done((f32[7,2048]{1,0:T(8,128)S(1)}, f32[7,2048]{1,0:T(8,128)S(1)}, u32[]{:S(2)}, u32[]{:S(2)}) %collective-permute-start.9) | collective-permute-done | bytes 57376 | tf_op jit(solution)/shard_map/ppermute | solution.py:26
  290.1 32.7 %collective-permute-done.10 = f32[7,2048]{1,0:T(8,128)S(1)} collective-permute-done((f32[7,2048]{1,0:T(8,128)S(1)}, f32[7,2048]{1,0:T(8,128)S(1)}, u32[]{:S(2)}, u32[]{:S(2)}) %collective-permute-start.10) | collective-permute-done | bytes 57376 | tf_op jit(solution)/shard_map/ppermute | solution.py:26
  322.8 3.0 collective-permute-start.11
  325.9 17.1 %fusion.20 = bf16[16,128,128]{2,1,0:T(8,128)(2,1)S(1)} fusion(bf16[16,2048,128]{2,1,0:T(8,128)(2,1)} %all-gather.4.cloned.1.call-done, f32[16,128,2048]{1,2,0:T(8,128)} %get-tuple-element.66, f32[16,128]{1,0:T(8,128)S(1)} %get-tuple-element.46, f32[16,2048,128]{2,1,0:T(8,128)} %get-tuple-element.65, f32[16,128]{1,0:T(8,128)S(1)} %fusion.5, ...), kind=kOutput, calls=%fused_computation.37 | convolution fusion | flops 1107558400 | bytes 42754048 | tf_op jit(solution)/shard_map/htu,hud->thd/dot_general | solution.py:101
  350.5 5.8 %fusion.50 = bf16[1,128,2048]{1,2,0:T(8,128)(2,1)S(1)} fusion(f32[2048]{0:T(1024)S(1)} %bitcast.157, f32[2048]{0:T(1024)S(1)} %bitcast.159, f32[2048]{0:T(1024)S(1)} %bitcast.149, bf16[128,2048]{0,1:T(8,128)(2,1)S(1)} %bitcast.131, f32[2048]{0:T(1024)S(1)} %bitcast.151, f32[2048]{0:T(1024)S(1)} %bitcast.153, f32[2048]{0:T(1024)S(1)} %bitcast.155, ...), kind=kLoop, calls=%fused_computation.93 | loop fusion | flops 10223616 | bytes 1130496 | tf_op jit(solution)/shard_map/broadcast_in_dim | solution.py:135
  357.3 6.0 %collective-permute-start.14 = (f32[7,2048]{1,0:T(8,128)S(1)}, f32[7,2048]{1,0:T(8,128)S(1)}, u32[]{:S(2)}, u32[]{:S(2)}) collective-permute-start(f32[7,2048]{1,0:T(8,128)S(1)} %add.89), channel_id=1, source_target_pairs={{0,64},{1,65},{2,66},{3,67},{4,68},{5,69},{6,70},{7,71},{8,72},{9,... | collective-permute-start | bytes 172040 | tf_op jit(solution)/shard_map/ppermute | solution.py:26
  365.8 6.2 %collective-permute-start.15 = (f32[7,2048]{1,0:T(8,128)S(1)}, f32[7,2048]{1,0:T(8,128)S(1)}, u32[]{:S(2)}, u32[]{:S(2)}) collective-permute-start(f32[7,2048]{1,0:T(8,128)S(1)} %add.90), channel_id=1, source_target_pairs={{0,128},{1,129},{2,130},{3,131},{4,132},{5,133},{6,134},{7,135},{8... | collective-permute-start | bytes 172040 | tf_op jit(solution)/shard_map/ppermute | solution.py:26
  372.1 14.8 %fusion = f32[16,128,2048]{1,2,0:T(8,128)} fusion(f32[16,2048]{1,0:T(8,128)S(1)} %get-tuple-element.53, f32[16,2048]{1,0:T(8,128)S(1)} %get-tuple-element.54, pred[128,2048]{0,1:T(8,128)(4,1)S(1)} %copy-done.2, bf16[16,2048,128]{2,1,0:T(8,128)(2,1)} %all-gather.8.cloned.1.call-done, bf16[128,16,128]{2,1,0:T(8,128)(2,1)S(1)} %bitcast.136), kind=kOutput, calls=%fused_computation.1 | convolution fusion | flops 1090519040 | bytes 26214400 | tf_op jit(solution)/shard_map/hud,htd->hut/dot_general | solution.py:112
  387.5 10.3 %copy.99 = bf16[16,16,128,128]{3,2,1,0:T(8,128)(2,1)} copy(bf16[16,16,128,128]{3,2,0,1:T(8,128)(2,1)} %bitcast.40) | data formatting | bytes 16777216 | tf_op jit(solution)/shard_map/reshape | solution.py:95
  397.9 11.0 %fusion.16 = bf16[16,128,128]{2,1,0:T(8,128)(2,1)S(1)} fusion(bf16[16,2048,128]{2,1,0:T(8,128)(2,1)} %bitcast.125, f32[16,128,2048]{1,2,0:T(8,128)} %fusion), kind=kOutput, calls=%fused_computation.34 | convolution fusion | flops 1078198272 | bytes 25690112 | tf_op jit(solution)/shard_map/hut,htd->uhd/dot_general | solution.py:121
  408.9 13.4 %fusion.19 = bf16[16,128,128]{2,1,0:T(8,128)(2,1)S(1)} fusion(bf16[16,2048,128]{2,1,0:T(8,128)(2,1)} %all-gather.8.cloned.1.call-done, f32[16,128,2048]{1,2,0:T(8,128)} %fusion, f32[16,2048]{1,0:T(8,128)S(1)} %get-tuple-element.52, bf16[16,2048,128]{2,1,0:T(8,128)(2,1)} %bitcast.126, bf16[128,16,128]{2,0,1:T(8,128)(2,1)S(1)} %copy-done), kind=kOutput, calls=%fused_computation.35 | convolution fusion | flops 2164523008 | bytes 34734080 | tf_op jit(solution)/shard_map/hut,htd->uhd/dot_general | solution.py:120
  (77 shorter events, 37.8 us)
Async XLA Ops:
  7.2 60.7 %all-gather.4.cloned.1.call-start = ((), (), s32[]{:S(2)}) async-start(), calls=%async_computation.1 | async-start | bytes 8912896 | tf_op jit(solution)/shard_map/all_gather | solution.py:70
  9.3 127.8 %all-gather.6.cloned.1.call-start = ((), (), s32[]{:S(2)}) async-start(), calls=%async_computation.2 | async-start | bytes 8912896 | tf_op jit(solution)/shard_map/all_gather | solution.py:72
  68.9 303.1 %all-gather.8.cloned.1.call-start = ((), (), s32[]{:S(2)}) async-start(), calls=%async_computation.3 | async-start | bytes 8912896 | tf_op jit(solution)/shard_map/all_gather | solution.py:85
  72.5 12.8 %copy-start.1 = (bf16[1,128,2048]{2,1,0:T(8,128)(2,1)S(1)}, bf16[1,128,2048]{2,1,0:T(8,128)(2,1)}, u32[]{:S(2)}) copy-start(bf16[1,128,2048]{2,1,0:T(8,128)(2,1)} %param.8) | copy-start | bytes 1572868
  72.5 17.0 %copy-start.3 = (f32[7,2048]{1,0:T(8,128)S(1)}, f32[7,2048]{1,0:T(8,128)}, u32[]{:S(2)}) copy-start(f32[7,2048]{1,0:T(8,128)} %param.9) | copy-start | bytes 172036
  86.6 20.9 %collective-permute-start.1 = (bf16[3,2048]{0,1:T(8,128)(2,1)}, bf16[3,2048]{0,1:T(8,128)(2,1)S(1)}, u32[]{:S(2)}, u32[]{:S(2)}) collective-permute-start(bf16[3,2048]{0,1:T(8,128)(2,1)} %get-tuple-element.51), channel_id=1, source_target_pairs={{0,1},{1,2},{2,3},{3,4},{4,5},{5,6},{6,7},{7,8},{8,9},{9,10},{10,1... | collective-permute-start | bytes 36872 | tf_op jit(solution)/shard_map/ppermute | solution.py:15
  86.9 20.7 %collective-permute-start = (bf16[3,2048]{0,1:T(8,128)(2,1)S(1)}, bf16[3,2048]{0,1:T(8,128)(2,1)}, u32[]{:S(2)}, u32[]{:S(2)}) collective-permute-start(bf16[3,2048]{0,1:T(8,128)(2,1)S(1)} %get-tuple-element.50), channel_id=1, source_target_pairs={{1,0},{2,1},{3,2},{4,3},{5,4},{6,5},{7,6},{8,7},{9,8},{10,9},{11,1... | collective-permute-start | bytes 36872 | tf_op jit(solution)/shard_map/ppermute | solution.py:16
  161.8 16.6 %collective-permute-start.2 = (bf16[3,2048]{1,0:T(4,128)(2,1)S(1)}, bf16[3,2048]{1,0:T(4,128)(2,1)S(1)}, u32[]{:S(2)}, u32[]{:S(2)}) collective-permute-start(bf16[3,2048]{1,0:T(4,128)(2,1)S(1)} %get-tuple-element.49), channel_id=1, source_target_pairs={{0,1},{1,2},{2,3},{3,4},{4,5},{5,6},{6,7},{7,8},{8,9},{9,10},{10,1... | collective-permute-start | bytes 36872 | tf_op jit(solution)/shard_map/ppermute | solution.py:15
  163.2 22.8 %collective-permute-start.3 = (bf16[3,2048]{0,1:T(8,128)(2,1)}, bf16[3,2048]{0,1:T(8,128)(2,1)}, u32[]{:S(2)}, u32[]{:S(2)}) collective-permute-start(bf16[3,2048]{0,1:T(8,128)(2,1)} %copy.91), channel_id=1, source_target_pairs={{1,0},{2,1},{3,2},{4,3},{5,4},{6,5},{7,6},{8,7},{9,8},{10,9},{11,1... | collective-permute-start | bytes 36872 | tf_op jit(solution)/shard_map/ppermute | solution.py:16
  172.0 215.6 %all-to-all-start = ((bf16[16,16,128,128]{3,2,1,0:T(8,128)(2,1)}), bf16[16,16,128,128]{3,2,1,0:T(8,128)(2,1)}, u32[]{:S(2)}, u32[]{:S(2)}) async-start(bf16[16,16,128,128]{3,2,1,0:T(8,128)(2,1)} %stack.21), calls=%async_computation | async-start | bytes 16777216 | tf_op jit(solution)/shard_map/all_to_all | solution.py:94
  190.9 22.8 %collective-permute-start.8 = (f32[7,2048]{1,0:T(8,128)S(1)}, f32[7,2048]{1,0:T(8,128)S(1)}, u32[]{:S(2)}, u32[]{:S(2)}) collective-permute-start(f32[7,2048]{1,0:T(8,128)S(1)} %stack.55), channel_id=1, source_target_pairs={{0,1},{1,0},{2,3},{3,2},{4,5},{5,4},{6,7},{7,6},{8,9},{9,8},{10,11... | collective-permute-start | bytes 172040 | tf_op jit(solution)/shard_map/ppermute | solution.py:26
  212.8 1.2 collective-permute-start.4
  213.7 74.2 %collective-permute-start.9 = (f32[7,2048]{1,0:T(8,128)S(1)}, f32[7,2048]{1,0:T(8,128)S(1)}, u32[]{:S(2)}, u32[]{:S(2)}) collective-permute-start(f32[7,2048]{1,0:T(8,128)S(1)} %add.84), channel_id=1, source_target_pairs={{0,2},{1,3},{2,0},{3,1},{4,6},{5,7},{6,4},{7,5},{8,10},{9,11},{10,... | collective-permute-start | bytes 172040 | tf_op jit(solution)/shard_map/ppermute | solution.py:26
  214.0 74.8 %collective-permute-start.5 = (f32[256,3,16]{0,2,1:T(8,128)S(1)}, f32[256,3,16]{0,2,1:T(8,128)S(1)}, u32[]{:S(2)}, u32[]{:S(2)}) collective-permute-start(f32[256,3,16]{0,2,1:T(8,128)S(1)} %maximum_select_fusion.3), channel_id=1, source_target_pairs={{0,2},{1,3},{2,0},{3,1},{4,6},{5,7},{6,4},{7,5},{8,10},{9,11},{10,... | collective-permute-start | bytes 147464 | tf_op jit(solution)/shard_map/ppermute | solution.py:37
  287.9 34.9 %collective-permute-start.10 = (f32[7,2048]{1,0:T(8,128)S(1)}, f32[7,2048]{1,0:T(8,128)S(1)}, u32[]{:S(2)}, u32[]{:S(2)}) collective-permute-start(f32[7,2048]{1,0:T(8,128)S(1)} %add.85), channel_id=1, source_target_pairs={{0,4},{1,5},{2,6},{3,7},{4,0},{5,1},{6,2},{7,3},{8,12},{9,13},{10,... | collective-permute-start | bytes 172040 | tf_op jit(solution)/shard_map/ppermute | solution.py:26
  288.8 56.2 %collective-permute-start.6 = (f32[512,3,16]{0,2,1:T(8,128)S(1)}, f32[512,3,16]{0,2,1:T(8,128)S(1)}, u32[]{:S(2)}, u32[]{:S(2)}) collective-permute-start(f32[512,3,16]{0,2,1:T(8,128)S(1)} %maximum_select_fusion.2), channel_id=1, source_target_pairs={{0,4},{1,5},{2,6},{3,7},{4,0},{5,1},{6,2},{7,3},{8,12},{9,13},{10,... | collective-permute-start | bytes 294920 | tf_op jit(solution)/shard_map/ppermute | solution.py:37
  322.8 21.1 %collective-permute-start.11 = (f32[7,2048]{1,0:T(8,128)S(1)}, f32[7,2048]{1,0:T(8,128)S(1)}, u32[]{:S(2)}, u32[]{:S(2)}) collective-permute-start(f32[7,2048]{1,0:T(8,128)S(1)} %add.86), channel_id=1, source_target_pairs={{0,8},{1,9},{2,10},{3,11},{4,12},{5,13},{6,14},{7,15},{8,0},{9,1},... | collective-permute-start | bytes 172040 | tf_op jit(solution)/shard_map/ppermute | solution.py:26
  325.9 46.2 %copy-start.2 = (pred[128,2048]{0,1:T(8,128)(4,1)S(1)}, pred[128,2048]{0,1:T(8,128)(4,1)}, u32[]{:S(2)}) copy-start(pred[128,2048]{0,1:T(8,128)(4,1)} %get-tuple-element.62) | copy-start | bytes 786436
  344.0 4.4 %collective-permute-start.12 = (f32[7,2048]{1,0:T(8,128)S(1)}, f32[7,2048]{1,0:T(8,128)S(1)}, u32[]{:S(2)}, u32[]{:S(2)}) collective-permute-start(f32[7,2048]{1,0:T(8,128)S(1)} %add.87), channel_id=1, source_target_pairs={{0,16},{1,17},{2,18},{3,19},{4,20},{5,21},{6,22},{7,23},{8,24},{9,... | collective-permute-start | bytes 172040 | tf_op jit(solution)/shard_map/ppermute | solution.py:26
  345.0 18.3 %collective-permute-start.7 = (f32[1024,3,16]{0,2,1:T(8,128)S(1)}, f32[1024,3,16]{0,2,1:T(8,128)S(1)}, u32[]{:S(2)}, u32[]{:S(2)}) collective-permute-start(f32[1024,3,16]{0,2,1:T(8,128)S(1)} %maximum_select_fusion.1), channel_id=1, source_target_pairs={{0,8},{1,9},{2,10},{3,11},{4,12},{5,13},{6,14},{7,15},{8,0},{9,1},... | collective-permute-start | bytes 589832 | tf_op jit(solution)/shard_map/ppermute | solution.py:37
  348.4 9.0 %collective-permute-start.13 = (f32[7,2048]{1,0:T(8,128)S(1)}, f32[7,2048]{1,0:T(8,128)S(1)}, u32[]{:S(2)}, u32[]{:S(2)}) collective-permute-start(f32[7,2048]{1,0:T(8,128)S(1)} %add.88), channel_id=1, source_target_pairs={{0,32},{1,33},{2,34},{3,35},{4,36},{5,37},{6,38},{7,39},{8,40},{9,... | collective-permute-start | bytes 172040 | tf_op jit(solution)/shard_map/ppermute | solution.py:26
  357.3 8.5 %collective-permute-start.14 = (f32[7,2048]{1,0:T(8,128)S(1)}, f32[7,2048]{1,0:T(8,128)S(1)}, u32[]{:S(2)}, u32[]{:S(2)}) collective-permute-start(f32[7,2048]{1,0:T(8,128)S(1)} %add.89), channel_id=1, source_target_pairs={{0,64},{1,65},{2,66},{3,67},{4,68},{5,69},{6,70},{7,71},{8,72},{9,... | collective-permute-start | bytes 172040 | tf_op jit(solution)/shard_map/ppermute | solution.py:26
  365.8 21.1 %collective-permute-start.15 = (f32[7,2048]{1,0:T(8,128)S(1)}, f32[7,2048]{1,0:T(8,128)S(1)}, u32[]{:S(2)}, u32[]{:S(2)}) collective-permute-start(f32[7,2048]{1,0:T(8,128)S(1)} %add.90), channel_id=1, source_target_pairs={{0,128},{1,129},{2,130},{3,131},{4,132},{5,133},{6,134},{7,135},{8... | collective-permute-start | bytes 172040 | tf_op jit(solution)/shard_map/ppermute | solution.py:26
  397.9 11.0 %copy-start = (bf16[128,16,128]{2,0,1:T(8,128)(2,1)S(1)}, bf16[128,16,128]{2,0,1:T(8,128)(2,1)}, u32[]{:S(2)}) copy-start(bf16[128,16,128]{2,0,1:T(8,128)(2,1)} %copy.82) | copy-start | bytes 1572868
Sparse Core Ops, SparseCore 0:
  10.4 57.4 all-gather.3
  70.3 66.7 all-gather.5
  138.9 146.4 all-gather.7
